TPU v7x, 512 devices: a whole 4x8x8 slice. The times are simulated.
512 devices in a mesh: grid: 64 (over x, z, core), orb: 8 (over y).
Axes of the slice: x: 4, y: 8, z: 8, core: 2. Of those that a mesh axis runs over, the one named last changes fastest.
Arguments:
- orbitals: float32 [256, 16, 16, 1024], P('grid', None, None, 'orb'), may hold values from -15 to 15
- potential: float32 [256, 16, 16], P('grid'), may hold values from -2 to 0
Outputs:
- filtered: float32 [256, 16, 16, 1024], P('grid', None, None, 'orb')
- hamiltonian_block: float32 [1024, 1024], P('orb', 'grid')
- margin_block: float32 [1024, 1024], P('orb', 'grid')
All inputs are finite; a program needn't handle non-finite values.
Results may differ from a plain program's by a relative error of at most 0.0039.
Values may be sent and summed in bfloat16 or wider, within the bound.
No kernel may reach another device: no remote copies, remote signals or barrier semaphores. Data moves between devices by JAX's collectives and lax.ppermute only.
A program may use at most 64 MiB of HBM per device.

v0:
```python
import jax
import jax.numpy as jnp
from jax import lax
from jax.sharding import PartitionSpec as P

DEGREE = 4
STENCIL = (-205.0 / 72.0, 8.0 / 5.0, -1.0 / 5.0, 8.0 / 315.0, -1.0 / 560.0)
LOWER_EDGE = -2.0
CUT_EDGE = 1.5
UPPER_EDGE = 10.0
EPSILON = 1e-06


def padded_2(shard, sides, width):
    for axis, dim in sides:
        size, length = (lax.axis_size(axis), shard.shape[dim])
        up = [(i, (i + 1) % size) for i in range(size - 1)]
        down = [(j, i) for i, j in up]
        last = lax.slice_in_dim(shard, length - width, length, axis=dim)
        initial = lax.slice_in_dim(shard, 0, width, axis=dim)
        before = lax.ppermute(last, axis, up)
        after = lax.ppermute(initial, axis, down)
        shard = jnp.concatenate([before, shard, after], axis=dim)
    return shard


def plane_matrix(rows_y, cols_x):
    flat_count = rows_y * cols_x
    index_all = jnp.arange(flat_count, dtype=jnp.int32)
    row_y = (index_all // cols_x)[:, None]
    row_x = (index_all % cols_x)[:, None]
    col_y = (index_all // cols_x)[None, :]
    col_x = (index_all % cols_x)[None, :]
    delta_y = jnp.mod(row_y - col_y, rows_y)
    delta_x = jnp.mod(row_x - col_x, cols_x)
    same_y = delta_y == 0
    same_x = delta_x == 0
    matrix = jnp.zeros((flat_count, flat_count), jnp.float32)
    for offset in range(1, 5):
        for signed in (offset, -offset):
            hit_y = jnp.logical_and(same_x, delta_y == signed % rows_y)
            hit_x = jnp.logical_and(same_y, delta_x == signed % cols_x)
            matrix = matrix + STENCIL[offset] * (
                hit_y.astype(jnp.float32) + hit_x.astype(jnp.float32)
            )
    return matrix


def apply_hamiltonian(current, potential, plane):
    layers, rows_y, cols_x, width = current.shape
    padded = padded_2(current.astype(jnp.bfloat16), (("grid", 0),), 4).astype(current.dtype)
    laplacian = 3.0 * STENCIL[0] * current
    for offset in range(1, 5):
        laplacian = laplacian + STENCIL[offset] * (
            padded[4 + offset : 4 + offset + layers] + padded[4 - offset : 4 - offset + layers]
        )
    flat = current.reshape(layers, rows_y * cols_x, width)
    in_plane = jnp.einsum(
        "pq,zqo->zpo",
        plane,
        flat,
        precision=lax.Precision.HIGHEST,
        preferred_element_type=jnp.float32,
    )
    laplacian = laplacian + in_plane.reshape(current.shape)
    return -0.5 * laplacian + potential[:, :, :, None] * current


def chebyshev(initial, potential, plane):
    half_width = (UPPER_EDGE - CUT_EDGE) / 2.0
    centre = (UPPER_EDGE + CUT_EDGE) / 2.0
    sigma_now = half_width / (LOWER_EDGE - centre)
    gamma_ratio = 2.0 / sigma_now
    previous = initial
    current = (
        sigma_now / half_width * (apply_hamiltonian(previous, potential, plane) - centre * previous)
    )
    for degree_step in range(DEGREE - 1):
        sigma_next = 1.0 / (gamma_ratio - sigma_now)
        following = (
            2.0
            * sigma_next
            / half_width
            * (apply_hamiltonian(current, potential, plane) - centre * current)
            - sigma_now * sigma_next * previous
        )
        previous, current, sigma_now = (current, following, sigma_next)
    return current


def contract_points(left_side, right_side):
    return lax.dot_general(
        left_side, right_side, (((0,), (0,)), ((), ())), preferred_element_type=jnp.float32
    )


def on_device(orbitals, potential):
    own_width = orbitals.shape[3]
    point_count = orbitals.shape[0] * orbitals.shape[1] * orbitals.shape[2]
    point_total = float(point_count * lax.axis_size("grid"))
    plane = plane_matrix(orbitals.shape[1], orbitals.shape[2])
    result_block = chebyshev(orbitals, potential, plane)
    own_squares = jnp.sum(result_block * result_block, axis=(0, 1, 2))
    rounded_orbitals = result_block.astype(jnp.bfloat16).reshape(point_count, own_width)
    rounded_image = (
        apply_hamiltonian(result_block, potential, plane)
        .astype(jnp.bfloat16)
        .reshape(point_count, own_width)
    )
    summed_own = lax.psum(own_squares, "grid")
    squares_all = lax.all_gather(summed_own, "orb", axis=0, tiled=True)
    scale_all = 1.0 / jnp.sqrt(squares_all / point_total + EPSILON)
    scale_own = lax.dynamic_slice_in_dim(scale_all, lax.axis_index("orb") * own_width, own_width)
    filtered = result_block * scale_own
    orbitals_all, images_all = (
        lax.all_gather(rounded_orbitals, "orb", axis=1, tiled=True),
        lax.all_gather(rounded_image, "orb", axis=1, tiled=True),
    )
    hamiltonian_part = contract_points(images_all, rounded_orbitals)
    margin_part = contract_points(orbitals_all, rounded_orbitals)
    combined = lax.psum_scatter(
        jnp.concatenate([hamiltonian_part, margin_part], axis=1),
        "grid",
        scatter_dimension=0,
        tiled=True,
    )
    column_count = combined.shape[0]
    column_scale = lax.dynamic_slice_in_dim(
        scale_all, lax.axis_index("grid") * column_count, column_count
    )
    pair_scale = scale_own[:, None] * column_scale[None, :] / point_total
    hamiltonian_block = combined[:, :own_width].T * pair_scale
    margin_block = combined[:, own_width:].T * pair_scale
    return (filtered, hamiltonian_block, margin_block)


def solution(mesh):
    placed = (P("grid", None, None, "orb"), P("grid", None, None))
    return jax.shard_map(
        on_device,
        mesh=mesh,
        in_specs=placed,
        out_specs=(P("grid", None, None, "orb"), P("orb", "grid"), P("orb", "grid")),
        check_vma=False,
    )
```

profile of v0, /device:TPU:8, one launch (start us, length us, event | category | flops | bytes accessed | tf_op | source)
XLA Modules:
  0.0 412.1 jit_solution(13175780743739567016)
XLA Ops:
  7.2 0.0 all-gather.6.cloned.1.call-start
  7.2 1.1 convert_element_type.210
  8.3 1.3 collective-permute-start.1
  9.6 3.0 collective-permute-start
  12.7 0.8 broadcast_multiply_fusion.2
  13.4 2.7 fusion.72
  16.1 0.0 copy-start.1
  16.1 0.0 copy-start.2
  16.1 0.0 collective-permute-done.1
  16.1 0.0 collective-permute-done
  16.1 0.1 maximum_convert_fusion
  16.3 0.9 copy-done.1
  17.1 0.4 fusion.155
  17.5 1.3 collective-permute-start.3
  18.8 4.5 %collective-permute-start.2 = (bf16[4,16,16,128]{3,2,1,0:T(8,128)(2,1)S(1)}, bf16[4,16,16,128]{3,2,1,0:T(8,128)(2,1)S(1)}, u32[]{:S(2)}, u32[]{:S(2)}) collective-permute-start(bf16[4,16,16,128]{3,2,1,0:T(8,128)(2,1)S(1)} %get-tuple-element.18), channel_id=1, source_target_pairs={{0,8},{8,16},{16,24},{24,32},{32,40},{40,48},{48,56},{56,64},{64,7... | collective-permute-start | bytes 786440 | tf_op jit(solution)/shard_map/ppermute | solution.py:21
  23.4 1.9 convolution_bitcast_fusion.3
  25.4 0.2 copy.26
  25.6 0.0 collective-permute-done.2
  25.6 0.1 maximum_convert_fusion.1
  25.7 0.4 fusion.160
  26.2 1.3 collective-permute-start.5
  27.5 5.3 %collective-permute-start.4 = (bf16[4,16,16,128]{3,2,1,0:T(8,128)(2,1)S(1)}, bf16[4,16,16,128]{3,2,1,0:T(8,128)(2,1)S(1)}, u32[]{:S(2)}, u32[]{:S(2)}) collective-permute-start(bf16[4,16,16,128]{3,2,1,0:T(8,128)(2,1)S(1)} %get-tuple-element.16), channel_id=1, source_target_pairs={{0,8},{8,16},{16,24},{24,32},{32,40},{40,48},{48,56},{56,64},{64,7... | collective-permute-start | bytes 786440 | tf_op jit(solution)/shard_map/ppermute | solution.py:21
  32.8 1.9 convolution_bitcast_fusion.2
  34.7 0.2 copy.28
  34.9 0.0 collective-permute-done.5
  35.0 0.0 collective-permute-done.4
  35.0 0.1 maximum_convert_fusion.2
  35.1 0.4 fusion.158
  35.5 1.3 collective-permute-start.7
  36.8 6.2 %collective-permute-start.6 = (bf16[4,16,16,128]{3,2,1,0:T(8,128)(2,1)S(1)}, bf16[4,16,16,128]{3,2,1,0:T(8,128)(2,1)S(1)}, u32[]{:S(2)}, u32[]{:S(2)}) collective-permute-start(bf16[4,16,16,128]{3,2,1,0:T(8,128)(2,1)S(1)} %get-tuple-element.14), channel_id=1, source_target_pairs={{0,8},{8,16},{16,24},{24,32},{32,40},{40,48},{48,56},{56,64},{64,7... | collective-permute-start | bytes 786440 | tf_op jit(solution)/shard_map/ppermute | solution.py:21
  43.0 1.9 convolution_bitcast_fusion.1
  44.9 0.2 copy.30
  45.1 0.0 collective-permute-done.6
  45.1 0.1 maximum_convert_fusion.3
  45.3 1.2 fusion.156
  46.4 0.0 all-gather.6.cloned.1.call-update
  46.4 0.0 all-gather.4.cloned.1.call-start
  46.5 1.3 collective-permute-start.9
  47.8 6.3 %collective-permute-start.8 = (bf16[4,16,16,128]{3,2,1,0:T(8,128)(2,1)}, bf16[4,16,16,128]{3,2,1,0:T(8,128)(2,1)S(1)}, u32[]{:S(2)}, u32[]{:S(2)}) collective-permute-start(bf16[4,16,16,128]{3,2,1,0:T(8,128)(2,1)} %get-tuple-element.12), channel_id=1, source_target_pairs={{0,8},{8,16},{16,24},{24,32},{32,40},{40,48},{48,56},{56,64},{64,7... | collective-permute-start | bytes 786440 | tf_op jit(solution)/shard_map/ppermute | solution.py:21
  54.1 1.9 convolution_bitcast_fusion
  56.1 0.2 multiply_reduce_fusion
  56.2 0.2 copy.32
  56.4 134.8 %psum.7 = f32[128]{0:T(128)S(1)} all-reduce(f32[128]{0:T(128)S(1)} %multiply_reduce_fusion), channel_id=1, replica_groups=mesh['grid'=64,'orb'=8] {'grid'}, use_global_device_ids=true, to_apply=%region_1.2 | all-reduce | flops 128 | bytes 1024 | tf_op jit(solution)/shard_map/psum | solution.py:110
  191.2 15.3 %all-gather = f32[8,1,128]{2,1,0:T(1,128)S(1)} all-gather(f32[1,1,128]{2,1,0:T(1,128)S(1)} %bitcast.65), channel_id=1, replica_groups=mesh['grid'=64,'orb'=8] {'orb'}, dimensions={0}, use_global_device_ids=true | all-gather | bytes 4608 | tf_op jit(solution)/shard_map/all_gather | solution.py:111
  206.5 0.1 dynamic_slice.6
  206.6 0.1 maximum_convert_fusion.4
  206.7 1.3 fusion.5
  208.0 0.0 all-gather.4.cloned.1.call-update
  208.0 0.0 reduce-scatter.4.cloned.1.call-start
  208.1 0.0 all-gather.6.cloned.1.call-done
  208.1 2.1 fusion.165
  210.2 39.9 %all-gather.4.cloned.1.call-done = bf16[1024,1024]{1,0:T(8,128)(2,1)} async-done(((bf16[1024,128]{1,0:T(8,128)(2,1)}), bf16[1024,1024]{1,0:T(8,128)(2,1)}) %all-gather.4.cloned.1.call-update) | async-done | bytes 2097168 | tf_op jit(solution)/shard_map/all_gather | solution.py:117
  250.1 2.1 fusion.164
  252.1 0.1 pad_maximum_fusion
  252.2 1.3 copy.39
  253.6 0.0 reduce-scatter.4.cloned.1.call-update
  253.6 0.1 dynamic_slice.7
  253.7 149.6 %reduce-scatter.4.cloned.1.call-done = f32[16,256]{1,0:T(8,128)} async-done(((f32[1024,256]{1,0:T(8,128)}), f32[16,256]{1,0:T(8,128)}) %reduce-scatter.4.cloned.1.call-update) | async-done | bytes 16400
  403.3 0.7 fusion.163
  404.0 0.1 copy.42
  404.1 0.1 copy.41
  404.2 0.1 bitcast_multiply_fusion
  404.3 0.7 copy.33
  404.9 0.7 copy.34
  (10 shorter events, 0.1 us)
Async XLA Ops:
  7.2 200.9 %all-gather.6.cloned.1.call-start = ((), (), s32[]{:S(2)}) async-start(), calls=%async_computation.2 | async-start | bytes 2359296 | tf_op jit(solution)/shard_map/all_gather | solution.py:116
  8.3 7.8 %collective-permute-start.1 = (bf16[4,16,16,128]{3,2,1,0:T(8,128)(2,1)S(1)}, bf16[4,16,16,128]{3,2,1,0:T(8,128)(2,1)S(1)}, u32[]{:S(2)}, u32[]{:S(2)}) collective-permute-start(bf16[4,16,16,128]{3,2,1,0:T(8,128)(2,1)S(1)} %convert_element_type.210), channel_id=1, source_target_pairs={{8,0},{16,8},{24,16},{32,24},{40,32},{48,40},{56,48},{64,56},{72,6... | collective-permute-start | bytes 786440 | tf_op jit(solution)/shard_map/ppermute | solution.py:22
  9.6 6.5 %collective-permute-start = (bf16[4,16,16,128]{3,2,1,0:T(8,128)(2,1)S(1)}, bf16[4,16,16,128]{3,2,1,0:T(8,128)(2,1)S(1)}, u32[]{:S(2)}, u32[]{:S(2)}) collective-permute-start(bf16[4,16,16,128]{3,2,1,0:T(8,128)(2,1)S(1)} %convert_element_type.210), channel_id=1, source_target_pairs={{0,8},{8,16},{16,24},{24,32},{32,40},{40,48},{48,56},{56,64},{64,7... | collective-permute-start | bytes 786440 | tf_op jit(solution)/shard_map/ppermute | solution.py:21
  16.1 1.0 copy-start.1
  16.1 1.0 copy-start.2
  17.5 8.0 %collective-permute-start.3 = (bf16[4,16,16,128]{3,2,1,0:T(8,128)(2,1)S(1)}, bf16[4,16,16,128]{3,2,1,0:T(8,128)(2,1)S(1)}, u32[]{:S(2)}, u32[]{:S(2)}) collective-permute-start(bf16[4,16,16,128]{3,2,1,0:T(8,128)(2,1)S(1)} %get-tuple-element.18), channel_id=1, source_target_pairs={{8,0},{16,8},{24,16},{32,24},{40,32},{48,40},{56,48},{64,56},{72,6... | collective-permute-start | bytes 786440 | tf_op jit(solution)/shard_map/ppermute | solution.py:22
  18.8 6.7 %collective-permute-start.2 = (bf16[4,16,16,128]{3,2,1,0:T(8,128)(2,1)S(1)}, bf16[4,16,16,128]{3,2,1,0:T(8,128)(2,1)S(1)}, u32[]{:S(2)}, u32[]{:S(2)}) collective-permute-start(bf16[4,16,16,128]{3,2,1,0:T(8,128)(2,1)S(1)} %get-tuple-element.18), channel_id=1, source_target_pairs={{0,8},{8,16},{16,24},{24,32},{32,40},{40,48},{48,56},{56,64},{64,7... | collective-permute-start | bytes 786440 | tf_op jit(solution)/shard_map/ppermute | solution.py:21
  26.2 8.8 %collective-permute-start.5 = (bf16[4,16,16,128]{3,2,1,0:T(8,128)(2,1)S(1)}, bf16[4,16,16,128]{3,2,1,0:T(8,128)(2,1)S(1)}, u32[]{:S(2)}, u32[]{:S(2)}) collective-permute-start(bf16[4,16,16,128]{3,2,1,0:T(8,128)(2,1)S(1)} %get-tuple-element.16), channel_id=1, source_target_pairs={{8,0},{16,8},{24,16},{32,24},{40,32},{48,40},{56,48},{64,56},{72,6... | collective-permute-start | bytes 786440 | tf_op jit(solution)/shard_map/ppermute | solution.py:22
  27.5 7.5 %collective-permute-start.4 = (bf16[4,16,16,128]{3,2,1,0:T(8,128)(2,1)S(1)}, bf16[4,16,16,128]{3,2,1,0:T(8,128)(2,1)S(1)}, u32[]{:S(2)}, u32[]{:S(2)}) collective-permute-start(bf16[4,16,16,128]{3,2,1,0:T(8,128)(2,1)S(1)} %get-tuple-element.16), channel_id=1, source_target_pairs={{0,8},{8,16},{16,24},{24,32},{32,40},{40,48},{48,56},{56,64},{64,7... | collective-permute-start | bytes 786440 | tf_op jit(solution)/shard_map/ppermute | solution.py:21
  35.5 9.6 %collective-permute-start.7 = (bf16[4,16,16,128]{3,2,1,0:T(8,128)(2,1)S(1)}, bf16[4,16,16,128]{3,2,1,0:T(8,128)(2,1)S(1)}, u32[]{:S(2)}, u32[]{:S(2)}) collective-permute-start(bf16[4,16,16,128]{3,2,1,0:T(8,128)(2,1)S(1)} %get-tuple-element.14), channel_id=1, source_target_pairs={{8,0},{16,8},{24,16},{32,24},{40,32},{48,40},{56,48},{64,56},{72,6... | collective-permute-start | bytes 786440 | tf_op jit(solution)/shard_map/ppermute | solution.py:22
  36.8 8.3 %collective-permute-start.6 = (bf16[4,16,16,128]{3,2,1,0:T(8,128)(2,1)S(1)}, bf16[4,16,16,128]{3,2,1,0:T(8,128)(2,1)S(1)}, u32[]{:S(2)}, u32[]{:S(2)}) collective-permute-start(bf16[4,16,16,128]{3,2,1,0:T(8,128)(2,1)S(1)} %get-tuple-element.14), channel_id=1, source_target_pairs={{0,8},{8,16},{16,24},{24,32},{32,40},{40,48},{48,56},{56,64},{64,7... | collective-permute-start | bytes 786440 | tf_op jit(solution)/shard_map/ppermute | solution.py:21
  46.4 203.6 %all-gather.4.cloned.1.call-start = ((), (), s32[]{:S(2)}) async-start(), calls=%async_computation.1 | async-start | bytes 2359296 | tf_op jit(solution)/shard_map/all_gather | solution.py:117
  46.5 160.1 %collective-permute-start.9 = (bf16[4,16,16,128]{3,2,1,0:T(8,128)(2,1)}, bf16[4,16,16,128]{3,2,1,0:T(8,128)(2,1)S(1)}, u32[]{:S(2)}, u32[]{:S(2)}) collective-permute-start(bf16[4,16,16,128]{3,2,1,0:T(8,128)(2,1)} %get-tuple-element.12), channel_id=1, source_target_pairs={{8,0},{16,8},{24,16},{32,24},{40,32},{48,40},{56,48},{64,56},{72,6... | collective-permute-start | bytes 786440 | tf_op jit(solution)/shard_map/ppermute | solution.py:22
  47.8 158.8 %collective-permute-start.8 = (bf16[4,16,16,128]{3,2,1,0:T(8,128)(2,1)}, bf16[4,16,16,128]{3,2,1,0:T(8,128)(2,1)S(1)}, u32[]{:S(2)}, u32[]{:S(2)}) collective-permute-start(bf16[4,16,16,128]{3,2,1,0:T(8,128)(2,1)} %get-tuple-element.12), channel_id=1, source_target_pairs={{0,8},{8,16},{16,24},{24,32},{32,40},{40,48},{48,56},{56,64},{64,7... | collective-permute-start | bytes 786440 | tf_op jit(solution)/shard_map/ppermute | solution.py:21
  56.1 150.5 %copy-start = (bf16[4,16,16,128]{3,2,1,0:T(8,128)(2,1)S(1)}, bf16[4,16,16,128]{3,2,1,0:T(8,128)(2,1)}, u32[]{:S(2)}) copy-start(bf16[4,16,16,128]{3,2,1,0:T(8,128)(2,1)} %get-tuple-element.12) | copy-start | bytes 786436
  208.0 195.2 %reduce-scatter.4.cloned.1.call-start = ((), (), s32[]{:S(2)}) async-start(), calls=%async_computation.3 | async-start | bytes 1064960
Sparse Core Ops, SparseCore 0:
  46.6 66.5 all-gather.5
  208.2 41.8 all-gather.3
  254.6 148.5 reduce-scatter.3
where the time goes:
time: 413 us; the launch traced here: 412 us
  waiting for transfers between devices  190 us (46%)
  blocking collectives  150 us (36%)
  starting transfers between devices  32 us (8%)
  matrix products  14.5 us (4%)
  between operations  14.1 us (3%)
  other arithmetic  6.55 us (2%)
  local copies, waits for them, and re-layouts  5.38 us (1%)
    unnamed x4, waiting for transfers between devices  150 us
    psum x1, blocking collectives, on_device(): summed_own = lax.psum(own_squares, 'grid')  135 us
    all_gather x1, waiting for transfers between devices, on_device(): lax.all_gather(rounded_image, 'orb', axis=1, tiled=True)  39.9 us
    ppermute x5, starting transfers between devices, padded_2(): before = lax.ppermute(last, axis, up)  25.4 us
    all_gather x1, blocking collectives, on_device(): squares_all = lax.all_gather(summed_own, 'orb', axis=0, tiled=True)  15.3 us
    dot_general x5, matrix products, apply_hamiltonian(): jnp.einsum('pq,zqo->zpo', plane, flat, precision=lax.Precision.HIGHEST, p...  10.4 us
  transfers between devices with their start and end apart: 13, of which 2 were waited for; matrix products, arithmetic and copies ran while one was open for 4% of the time, Pallas kernels for 0%

commit v1 on v0

--- a/solution.py
+++ b/solution.py
@@ -107,7 +107,7 @@
         .astype(jnp.bfloat16)
         .reshape(point_count, own_width)
     )
-    summed_own = lax.psum(own_squares, "grid")
+    summed_own = jnp.sum(lax.all_gather(own_squares, "grid"), 0)
     squares_all = lax.all_gather(summed_own, "orb", axis=0, tiled=True)
     scale_all = 1.0 / jnp.sqrt(squares_all / point_total + EPSILON)
     scale_own = lax.dynamic_slice_in_dim(scale_all, lax.axis_index("orb") * own_width, own_width)

time: 413 us -> 338 us (0.82)
  blocking collectives: 150 us -> 71.1 us
    psum x1 -> x0, blocking collectives: 135 us -> none  [on_device(): summed_own = lax.psum(own_squares, 'grid')]
    all_gather x0 -> x1, blocking collectives: none -> 55.8 us  [on_device(): summed_own = jnp.sum(lax.all_gather(own_squares, 'grid'), 0)]
    all_gather x1, waiting for transfers between devices: 39.9 us -> 44.3 us  [on_device(): lax.all_gather(rounded_image, 'orb', axis=1, tiled=True)]
  transfers between devices with their start and end apart: 13 -> 13, of which waited for: 2 -> 2; matrix products, arithmetic and copies ran while one was open for 4% -> 5% of each run, Pallas kernels for 0% -> 0%
where the time goes in v1:
time: 338 us
  waiting for transfers between devices  194 us (57%)
  blocking collectives  71.1 us (21%)
  starting transfers between devices  32 us (9%)
  matrix products  14.5 us (4%)
  between operations  14.1 us (4%)
  other arithmetic  6.63 us (2%)
  local copies, waits for them, and re-layouts  5.38 us (2%)
    unnamed x4, waiting for transfers between devices  150 us
    all_gather x1, blocking collectives, on_device(): summed_own = jnp.sum(lax.all_gather(own_squares, 'grid'), 0)  55.8 us
    all_gather x1, waiting for transfers between devices, on_device(): lax.all_gather(rounded_image, 'orb', axis=1, tiled=True)  44.3 us
    ppermute x5, starting transfers between devices, padded_2(): before = lax.ppermute(last, axis, up)  25.4 us
    all_gather x1, blocking collectives, on_device(): squares_all = lax.all_gather(summed_own, 'orb', axis=0, tiled=True)  15.3 us
    dot_general x5, matrix products, apply_hamiltonian(): jnp.einsum('pq,zqo->zpo', plane, flat, precision=lax.Precision.HIGHEST, p...  10.4 us
  transfers between devices with their start and end apart: 13, of which 2 were waited for; matrix products, arithmetic and copies ran while one was open for 5% of the time, Pallas kernels for 0%

profile of v1, /device:TPU:8, one launch (start us, length us, event | category | flops | bytes accessed | tf_op | source)
XLA Modules:
  0.0 337.8 jit_solution(11831510645152667847)
XLA Ops:
  7.2 0.0 all-gather.8.cloned.1.call-start
  7.2 1.1 convert_element_type.210
  8.3 1.3 collective-permute-start.1
  9.6 3.0 collective-permute-start
  12.7 0.8 broadcast_multiply_fusion.2
  13.4 2.7 fusion.72
  16.1 0.0 copy-start.1
  16.1 0.0 copy-start.2
  16.1 0.1 maximum_convert_fusion
  16.3 0.9 copy-done.1
  17.1 0.4 fusion.155
  17.5 1.3 collective-permute-start.3
  18.8 4.5 %collective-permute-start.2 = (bf16[4,16,16,128]{3,2,1,0:T(8,128)(2,1)S(1)}, bf16[4,16,16,128]{3,2,1,0:T(8,128)(2,1)S(1)}, u32[]{:S(2)}, u32[]{:S(2)}) collective-permute-start(bf16[4,16,16,128]{3,2,1,0:T(8,128)(2,1)S(1)} %get-tuple-element.18), channel_id=1, source_target_pairs={{0,8},{8,16},{16,24},{24,32},{32,40},{40,48},{48,56},{56,64},{64,7... | collective-permute-start | bytes 786440 | tf_op jit(solution)/shard_map/ppermute | solution.py:21
  23.4 1.9 convolution_bitcast_fusion.3
  25.4 0.2 copy.26
  25.6 0.0 collective-permute-done.2
  25.6 0.1 maximum_convert_fusion.1
  25.7 0.4 fusion.160
  26.2 1.3 collective-permute-start.5
  27.5 5.3 %collective-permute-start.4 = (bf16[4,16,16,128]{3,2,1,0:T(8,128)(2,1)S(1)}, bf16[4,16,16,128]{3,2,1,0:T(8,128)(2,1)S(1)}, u32[]{:S(2)}, u32[]{:S(2)}) collective-permute-start(bf16[4,16,16,128]{3,2,1,0:T(8,128)(2,1)S(1)} %get-tuple-element.16), channel_id=1, source_target_pairs={{0,8},{8,16},{16,24},{24,32},{32,40},{40,48},{48,56},{56,64},{64,7... | collective-permute-start | bytes 786440 | tf_op jit(solution)/shard_map/ppermute | solution.py:21
  32.8 1.9 convolution_bitcast_fusion.2
  34.7 0.2 copy.28
  34.9 0.0 collective-permute-done.5
  35.0 0.0 collective-permute-done.4
  35.0 0.1 maximum_convert_fusion.2
  35.1 0.4 fusion.158
  35.5 1.3 collective-permute-start.7
  36.8 6.2 %collective-permute-start.6 = (bf16[4,16,16,128]{3,2,1,0:T(8,128)(2,1)S(1)}, bf16[4,16,16,128]{3,2,1,0:T(8,128)(2,1)S(1)}, u32[]{:S(2)}, u32[]{:S(2)}) collective-permute-start(bf16[4,16,16,128]{3,2,1,0:T(8,128)(2,1)S(1)} %get-tuple-element.14), channel_id=1, source_target_pairs={{0,8},{8,16},{16,24},{24,32},{32,40},{40,48},{48,56},{56,64},{64,7... | collective-permute-start | bytes 786440 | tf_op jit(solution)/shard_map/ppermute | solution.py:21
  43.0 1.9 convolution_bitcast_fusion.1
  44.9 0.2 copy.30
  45.1 0.0 collective-permute-done.6
  45.1 0.1 maximum_convert_fusion.3
  45.3 1.2 fusion.156
  46.4 0.0 all-gather.8.cloned.1.call-update
  46.4 0.0 all-gather.6.cloned.1.call-start
  46.5 1.3 collective-permute-start.9
  47.8 6.3 %collective-permute-start.8 = (bf16[4,16,16,128]{3,2,1,0:T(8,128)(2,1)}, bf16[4,16,16,128]{3,2,1,0:T(8,128)(2,1)S(1)}, u32[]{:S(2)}, u32[]{:S(2)}) collective-permute-start(bf16[4,16,16,128]{3,2,1,0:T(8,128)(2,1)} %get-tuple-element.12), channel_id=1, source_target_pairs={{0,8},{8,16},{16,24},{24,32},{32,40},{40,48},{48,56},{56,64},{64,7... | collective-permute-start | bytes 786440 | tf_op jit(solution)/shard_map/ppermute | solution.py:21
  54.1 1.9 convolution_bitcast_fusion
  56.1 0.2 multiply_reduce_fusion
  56.2 0.2 copy.32
  56.4 55.8 %all-gather.1 = f32[64,1,128]{2,1,0:T(1,128)S(1)} all-gather(f32[1,1,128]{2,1,0:T(1,128)S(1)} %bitcast.66), channel_id=2, replica_groups=mesh['grid'=64,'orb'=8] {'grid'}, dimensions={0}, use_global_device_ids=true | all-gather | bytes 33280 | tf_op jit(solution)/shard_map/all_gather | solution.py:110
  112.3 0.1 reduce_sum.19
  112.4 15.3 %all-gather.2 = f32[8,1,128]{2,1,0:T(1,128)S(1)} all-gather(f32[1,1,128]{2,1,0:T(1,128)S(1)} %bitcast.67), channel_id=1, replica_groups=mesh['grid'=64,'orb'=8] {'orb'}, dimensions={0}, use_global_device_ids=true | all-gather | bytes 4608 | tf_op jit(solution)/shard_map/all_gather | solution.py:111
  127.7 0.1 dynamic_slice.6
  127.8 0.0 collective-permute-done.9
  127.8 0.1 maximum_convert_fusion.4
  127.9 1.3 fusion.5
  129.2 0.0 all-gather.6.cloned.1.call-update
  129.2 0.0 reduce-scatter.4.cloned.1.call-start
  129.2 0.0 all-gather.8.cloned.1.call-done
  129.3 2.1 fusion.165
  131.4 44.3 %all-gather.6.cloned.1.call-done = bf16[1024,1024]{1,0:T(8,128)(2,1)} async-done(((bf16[1024,128]{1,0:T(8,128)(2,1)}), bf16[1024,1024]{1,0:T(8,128)(2,1)}) %all-gather.6.cloned.1.call-update) | async-done | bytes 2097168 | tf_op jit(solution)/shard_map/all_gather | solution.py:117
  175.7 2.1 fusion.164
  177.8 0.1 pad_maximum_fusion
  177.9 1.3 copy.39
  179.2 0.0 reduce-scatter.4.cloned.1.call-update
  179.3 0.1 dynamic_slice.7
  179.3 149.6 %reduce-scatter.4.cloned.1.call-done = f32[16,256]{1,0:T(8,128)} async-done(((f32[1024,256]{1,0:T(8,128)}), f32[16,256]{1,0:T(8,128)}) %reduce-scatter.4.cloned.1.call-update) | async-done | bytes 16400
  328.9 0.7 fusion.163
  329.6 0.1 copy.42
  329.7 0.1 copy.41
  329.8 0.1 bitcast_multiply_fusion
  329.9 0.7 copy.33
  330.6 0.7 copy.34
  (11 shorter events, 0.1 us)
Async XLA Ops:
  7.2 122.1 %all-gather.8.cloned.1.call-start = ((), (), s32[]{:S(2)}) async-start(), calls=%async_computation.2 | async-start | bytes 2359296 | tf_op jit(solution)/shard_map/all_gather | solution.py:116
  8.3 7.8 %collective-permute-start.1 = (bf16[4,16,16,128]{3,2,1,0:T(8,128)(2,1)S(1)}, bf16[4,16,16,128]{3,2,1,0:T(8,128)(2,1)S(1)}, u32[]{:S(2)}, u32[]{:S(2)}) collective-permute-start(bf16[4,16,16,128]{3,2,1,0:T(8,128)(2,1)S(1)} %convert_element_type.210), channel_id=1, source_target_pairs={{8,0},{16,8},{24,16},{32,24},{40,32},{48,40},{56,48},{64,56},{72,6... | collective-permute-start | bytes 786440 | tf_op jit(solution)/shard_map/ppermute | solution.py:22
  9.6 6.5 %collective-permute-start = (bf16[4,16,16,128]{3,2,1,0:T(8,128)(2,1)S(1)}, bf16[4,16,16,128]{3,2,1,0:T(8,128)(2,1)S(1)}, u32[]{:S(2)}, u32[]{:S(2)}) collective-permute-start(bf16[4,16,16,128]{3,2,1,0:T(8,128)(2,1)S(1)} %convert_element_type.210), channel_id=1, source_target_pairs={{0,8},{8,16},{16,24},{24,32},{32,40},{40,48},{48,56},{56,64},{64,7... | collective-permute-start | bytes 786440 | tf_op jit(solution)/shard_map/ppermute | solution.py:21
  16.1 1.0 copy-start.1
  16.1 1.0 copy-start.2
  17.5 8.0 %collective-permute-start.3 = (bf16[4,16,16,128]{3,2,1,0:T(8,128)(2,1)S(1)}, bf16[4,16,16,128]{3,2,1,0:T(8,128)(2,1)S(1)}, u32[]{:S(2)}, u32[]{:S(2)}) collective-permute-start(bf16[4,16,16,128]{3,2,1,0:T(8,128)(2,1)S(1)} %get-tuple-element.18), channel_id=1, source_target_pairs={{8,0},{16,8},{24,16},{32,24},{40,32},{48,40},{56,48},{64,56},{72,6... | collective-permute-start | bytes 786440 | tf_op jit(solution)/shard_map/ppermute | solution.py:22
  18.8 6.7 %collective-permute-start.2 = (bf16[4,16,16,128]{3,2,1,0:T(8,128)(2,1)S(1)}, bf16[4,16,16,128]{3,2,1,0:T(8,128)(2,1)S(1)}, u32[]{:S(2)}, u32[]{:S(2)}) collective-permute-start(bf16[4,16,16,128]{3,2,1,0:T(8,128)(2,1)S(1)} %get-tuple-element.18), channel_id=1, source_target_pairs={{0,8},{8,16},{16,24},{24,32},{32,40},{40,48},{48,56},{56,64},{64,7... | collective-permute-start | bytes 786440 | tf_op jit(solution)/shard_map/ppermute | solution.py:21
  26.2 8.8 %collective-permute-start.5 = (bf16[4,16,16,128]{3,2,1,0:T(8,128)(2,1)S(1)}, bf16[4,16,16,128]{3,2,1,0:T(8,128)(2,1)S(1)}, u32[]{:S(2)}, u32[]{:S(2)}) collective-permute-start(bf16[4,16,16,128]{3,2,1,0:T(8,128)(2,1)S(1)} %get-tuple-element.16), channel_id=1, source_target_pairs={{8,0},{16,8},{24,16},{32,24},{40,32},{48,40},{56,48},{64,56},{72,6... | collective-permute-start | bytes 786440 | tf_op jit(solution)/shard_map/ppermute | solution.py:22
  27.5 7.5 %collective-permute-start.4 = (bf16[4,16,16,128]{3,2,1,0:T(8,128)(2,1)S(1)}, bf16[4,16,16,128]{3,2,1,0:T(8,128)(2,1)S(1)}, u32[]{:S(2)}, u32[]{:S(2)}) collective-permute-start(bf16[4,16,16,128]{3,2,1,0:T(8,128)(2,1)S(1)} %get-tuple-element.16), channel_id=1, source_target_pairs={{0,8},{8,16},{16,24},{24,32},{32,40},{40,48},{48,56},{56,64},{64,7... | collective-permute-start | bytes 786440 | tf_op jit(solution)/shard_map/ppermute | solution.py:21
  35.5 9.6 %collective-permute-start.7 = (bf16[4,16,16,128]{3,2,1,0:T(8,128)(2,1)S(1)}, bf16[4,16,16,128]{3,2,1,0:T(8,128)(2,1)S(1)}, u32[]{:S(2)}, u32[]{:S(2)}) collective-permute-start(bf16[4,16,16,128]{3,2,1,0:T(8,128)(2,1)S(1)} %get-tuple-element.14), channel_id=1, source_target_pairs={{8,0},{16,8},{24,16},{32,24},{40,32},{48,40},{56,48},{64,56},{72,6... | collective-permute-start | bytes 786440 | tf_op jit(solution)/shard_map/ppermute | solution.py:22
  36.8 8.3 %collective-permute-start.6 = (bf16[4,16,16,128]{3,2,1,0:T(8,128)(2,1)S(1)}, bf16[4,16,16,128]{3,2,1,0:T(8,128)(2,1)S(1)}, u32[]{:S(2)}, u32[]{:S(2)}) collective-permute-start(bf16[4,16,16,128]{3,2,1,0:T(8,128)(2,1)S(1)} %get-tuple-element.14), channel_id=1, source_target_pairs={{0,8},{8,16},{16,24},{24,32},{32,40},{40,48},{48,56},{56,64},{64,7... | collective-permute-start | bytes 786440 | tf_op jit(solution)/shard_map/ppermute | solution.py:21
  46.4 129.3 %all-gather.6.cloned.1.call-start = ((), (), s32[]{:S(2)}) async-start(), calls=%async_computation.1 | async-start | bytes 2359296 | tf_op jit(solution)/shard_map/all_gather | solution.py:117
  46.5 81.3 %collective-permute-start.9 = (bf16[4,16,16,128]{3,2,1,0:T(8,128)(2,1)}, bf16[4,16,16,128]{3,2,1,0:T(8,128)(2,1)S(1)}, u32[]{:S(2)}, u32[]{:S(2)}) collective-permute-start(bf16[4,16,16,128]{3,2,1,0:T(8,128)(2,1)} %get-tuple-element.12), channel_id=1, source_target_pairs={{8,0},{16,8},{24,16},{32,24},{40,32},{48,40},{56,48},{64,56},{72,6... | collective-permute-start | bytes 786440 | tf_op jit(solution)/shard_map/ppermute | solution.py:22
  47.8 80.0 %collective-permute-start.8 = (bf16[4,16,16,128]{3,2,1,0:T(8,128)(2,1)}, bf16[4,16,16,128]{3,2,1,0:T(8,128)(2,1)S(1)}, u32[]{:S(2)}, u32[]{:S(2)}) collective-permute-start(bf16[4,16,16,128]{3,2,1,0:T(8,128)(2,1)} %get-tuple-element.12), channel_id=1, source_target_pairs={{0,8},{8,16},{16,24},{24,32},{32,40},{40,48},{48,56},{56,64},{64,7... | collective-permute-start | bytes 786440 | tf_op jit(solution)/shard_map/ppermute | solution.py:21
  56.1 71.7 %copy-start = (bf16[4,16,16,128]{3,2,1,0:T(8,128)(2,1)S(1)}, bf16[4,16,16,128]{3,2,1,0:T(8,128)(2,1)}, u32[]{:S(2)}) copy-start(bf16[4,16,16,128]{3,2,1,0:T(8,128)(2,1)} %get-tuple-element.12) | copy-start | bytes 786436
  129.2 199.7 %reduce-scatter.4.cloned.1.call-start = ((), (), s32[]{:S(2)}) async-start(), calls=%async_computation.3 | async-start | bytes 1064960
Sparse Core Ops, SparseCore 0:
  46.6 66.1 all-gather.7
  129.3 46.3 all-gather.5
  180.3 148.5 reduce-scatter.3
